TPU v7x, 32 devices: a whole 2x2x4 slice. The times are simulated.
32 devices in a mesh: expert: 2 (over y), hidden: 16 (over z, x, core).
Axes of the slice: x: 2, y: 2, z: 4, core: 2. Of those that a mesh axis runs over, the one named last changes fastest.
Arguments:
- tokens: bfloat16 [192, 3072], P('expert', 'hidden'), may hold values from -6 to 6
- cotangent: bfloat16 [192, 3072], P('expert', 'hidden'), may hold values from -6 to 6
- w_gate: bfloat16 [2, 3072, 16384], P('expert', None, 'hidden'), may hold values from -0.15625 to 0.15625
- w_up: bfloat16 [2, 3072, 16384], P('expert', None, 'hidden'), may hold values from -0.15625 to 0.15625
- w_down: bfloat16 [2, 16384, 3072], P('expert', 'hidden'), may hold values from -0.046875 to 0.046875
- slot_token: int32 [2, 192], P(None, 'expert'), may hold values from 0 to 95, as said below
- slot_weight: float32 [2, 192], P(None, 'expert'), may hold values from 0.2 to 1
- keep_mask: int32 [2, 192, 16384], P('expert', None, 'hidden'), may hold values 0 or 1
Outputs:
- grad_tokens: bfloat16 [192, 3072], P('expert', 'hidden')
Inputs may be any that keep to these rules, and one draw needn't show every extreme that they name: `slot_token`: slots s of block g = s // 96 of every expert hold tokens of group g (token rows g * 96 to (g + 1) * 96 - 1); within one expert and one block the 96 entries are distinct; every slot is filled.
All inputs are finite; a program needn't handle non-finite values. No bound on the sum of `keep_mask` on one device may be relied on, other than what follows from the above.
Results may differ from a plain program's by a relative error of at most 0.012.
Values may be sent and summed in bfloat16 or wider, within the bound.
No kernel may reach another device: no remote copies, remote signals or barrier semaphores. Data moves between devices by JAX's collectives and lax.ppermute only.
A program may use at most 64 MiB of HBM per device.

v0:
```python
import jax
import jax.numpy as jnp
from jax import lax
from jax.sharding import PartitionSpec as P

keep_rate = 0.9


def gelu_tanh(values):
    return jax.nn.gelu(values, approximate=True)


def fold_slots(slot_values, one_hot):
    high_part = slot_values.astype(jnp.bfloat16)
    low_part = (slot_values - high_part.astype(jnp.float32)).astype(jnp.bfloat16)
    return jnp.dot(high_part, one_hot, preferred_element_type=jnp.float32) + jnp.dot(
        low_part, one_hot, preferred_element_type=jnp.float32
    )


def body(tokens, cotangent, w_gate, w_up, w_down, slot_token, slot_weight, keep_mask):
    gate_mat = w_gate[0]
    up_mat = w_up[0]
    down_mat = w_down[0]
    model_width = gate_mat.shape[0]
    expert_count = lax.axis_size("expert")
    expert_total = slot_token.shape[0]
    per_source = slot_token.shape[1]
    slot_count = expert_count * per_source
    group_tokens = tokens.shape[0]
    slot_list = slot_token.reshape(-1)
    weight_column = slot_weight.reshape(-1, 1)
    inv_keep = 1.0 / keep_rate
    chosen = tokens[slot_list].reshape(expert_total, per_source, -1)
    scaled = (weight_column * cotangent[slot_list].astype(jnp.float32)).astype(jnp.bfloat16)
    sent_cot = scaled.reshape(expert_total, per_source, -1)
    recv_inputs, recv_cot = (
        lax.all_to_all(chosen, "expert", split_axis=0, concat_axis=0, tiled=True),
        lax.all_to_all(sent_cot, "expert", split_axis=0, concat_axis=0, tiled=True),
    )
    slot_inputs = recv_inputs.reshape(slot_count, -1)
    slot_cot = recv_cot.reshape(slot_count, -1)
    part_inputs = lax.all_gather(slot_inputs, "hidden", axis=1, tiled=True)
    part_cot = lax.all_gather(slot_cot, "hidden", axis=1, tiled=True)
    gate_rows = gate_mat
    up_rows = up_mat
    gate_pre = jnp.dot(part_inputs, gate_rows, preferred_element_type=jnp.float32)
    up_pre = jnp.dot(part_inputs, up_rows, preferred_element_type=jnp.float32)
    grad_hidden = lax.dot_general(
        part_cot, down_mat, (((1,), (1,)), ((), ())), preferred_element_type=jnp.float32
    )
    activated, pullback = jax.vjp(gelu_tanh, gate_pre)
    grad_pre = grad_hidden * keep_mask[0].astype(jnp.float32) * inv_keep
    grad_up = (grad_pre * activated).astype(jnp.bfloat16)
    grad_gate = pullback(grad_pre * up_pre)[0].astype(jnp.bfloat16)
    one_hot = (slot_list[:, None] == jnp.arange(group_tokens, dtype=jnp.int32)[None, :]).astype(
        jnp.bfloat16
    )
    local_width = model_width // lax.axis_size("hidden")
    gate_rows = gate_mat
    up_rows = up_mat
    reduced = lax.psum_scatter(
        lax.dot_general(
            gate_rows, grad_gate, (((1,), (1,)), ((), ())), preferred_element_type=jnp.float32
        )
        + lax.dot_general(
            up_rows, grad_up, (((1,), (1,)), ((), ())), preferred_element_type=jnp.float32
        ),
        "hidden",
        scatter_dimension=0,
        tiled=True,
    )
    returned = lax.all_to_all(
        reduced.reshape(local_width, expert_count, per_source),
        "expert",
        split_axis=1,
        concat_axis=1,
        tiled=True,
    )
    token_sum = fold_slots(returned.reshape(local_width, -1), one_hot)
    return token_sum.T.astype(jnp.bfloat16)


def solution(mesh):
    in_specs = (
        P("expert", "hidden"),
        P("expert", "hidden"),
        P("expert", None, "hidden"),
        P("expert", None, "hidden"),
        P("expert", "hidden", None),
        P(None, "expert"),
        P(None, "expert"),
        P("expert", None, "hidden"),
    )
    out_specs = P("expert", "hidden")
    return jax.shard_map(body, mesh=mesh, in_specs=in_specs, out_specs=out_specs, check_vma=False)
```

profile of v0, /device:TPU:0, one launch (start us, length us, event | category | flops | bytes accessed | tf_op | source)
XLA Modules:
  0.0 205.2 jit_solution(17161815436193137995)
XLA Ops:
  6.5 0.0 copy-start
  6.5 0.0 all-gather.5.cloned.1.call-start
  6.5 0.8 reshape.59
  7.3 0.0 copy-done
  7.3 1.0 gather_fusion.1
  8.4 8.3 %all_to_all.15 = bf16[2,96,192]{2,1,0:T(8,128)(2,1)S(1)} all-to-all(bf16[2,96,192]{2,1,0:T(8,128)(2,1)S(1)} %bitcast.53), channel_id=1, replica_groups=mesh['expert'=2,'hidden'=16] {'expert'}, dimensions={0} | all-to-all | bytes 147456 | tf_op jit(solution)/shard_map/all_to_all | solution.py:38
  16.7 0.7 copy.12
  17.4 0.0 all-gather.5.cloned.1.call-update
  17.4 0.0 all-gather.3.cloned.1.call-start
  17.5 1.7 gather_fusion
  19.2 0.8 fusion.48
  19.9 6.7 %all_to_all.16 = bf16[2,96,192]{2,1,0:T(8,128)(2,1)S(1)} all-to-all(bf16[2,96,192]{2,1,0:T(8,128)(2,1)S(1)} %fusion.48), channel_id=1, replica_groups=mesh['expert'=2,'hidden'=16] {'expert'}, dimensions={0} | all-to-all | bytes 147456 | tf_op jit(solution)/shard_map/all_to_all | solution.py:39
  26.6 0.7 copy.11
  27.3 0.0 all-gather.3.cloned.1.call-update
  27.4 0.0 reduce-scatter.4.cloned.1.call-start
  27.4 30.1 %all-gather.5.cloned.1.call-done = bf16[192,3072]{0,1:T(8,128)(2,1)} async-done(((bf16[192,192]{0,1:T(8,128)(2,1)}), bf16[192,3072]{0,1:T(8,128)(2,1)}) %all-gather.5.cloned.1.call-update) | async-done | bytes 1179664 | tf_op jit(solution)/shard_map/all_gather | solution.py:43
  57.6 4.7 %fusion.2 = f32[192,1024]{1,0:T(8,128)S(1)} fusion(bf16[192,3072]{0,1:T(8,128)(2,1)} %all-gather.5.cloned.1.call-done, bf16[1,3072,1024]{2,1,0:T(8,128)(2,1)} %param.10), kind=kOutput, calls=%fused_computation.4 | convolution fusion | flops 1207959552 | bytes 8257536 | tf_op jit(solution)/shard_map/dot_general | solution.py:47
  62.3 0.0 copy-start.1
  62.3 36.2 %all-gather.3.cloned.1.call-done = bf16[192,3072]{0,1:T(8,128)(2,1)} async-done(((bf16[192,192]{0,1:T(8,128)(2,1)}), bf16[192,3072]{0,1:T(8,128)(2,1)}) %all-gather.3.cloned.1.call-update) | async-done | bytes 1179664 | tf_op jit(solution)/shard_map/all_gather | solution.py:44
  98.4 5.6 %fusion.22 = f32[192,1024]{1,0:T(8,128)S(1)} fusion(bf16[192,3072]{0,1:T(8,128)(2,1)} %all-gather.3.cloned.1.call-done, bf16[1,1024,3072]{2,1,0:T(8,128)(2,1)} %param.12, s32[1,192,1024]{2,1,0:T(8,128)} %param.15), kind=kOutput, calls=%fused_computation.16 | convolution fusion | flops 1208549376 | bytes 9043968 | tf_op jit(solution)/shard_map/dot_general | solution.py:49
  104.1 9.9 %fusion = f32[192,3072]{1,0:T(8,128)} fusion(bf16[1,3072,1024]{2,1,0:T(8,128)(2,1)} %param.10, f32[192,1024]{1,0:T(8,128)S(1)} %fusion.2, f32[192,1024]{1,0:T(8,128)S(1)} %fusion.22, bf16[192,3072]{0,1:T(8,128)(2,1)S(1)} %copy-done.1, bf16[1,3072,1024]{2,1,0:T(8,128)(2,1)} %param.11), kind=kOutput, calls=%fused_computation.2 | convolution fusion | flops 2420047872 | bytes 17694720 | tf_op jit(solution)/shard_map/dot_general | solution.py:63
  114.0 5.9 %fusion.13 = f32[3072,192]{0,1:T(8,128)S(1)} fusion(f32[192,3072]{1,0:T(8,128)} %fusion, bf16[1,3072,1024]{2,1,0:T(8,128)(2,1)} %param.11, f32[192,1024]{1,0:T(8,128)S(1)} %fusion.22, f32[192,1024]{1,0:T(8,128)} %copy-done.2), kind=kOutput, calls=%fused_computation.13 | convolution fusion | flops 1210515456 | bytes 12582912 | tf_op jit(solution)/shard_map/dot_general | solution.py:66
  120.0 0.0 copy-start.3
  120.0 2.3 %copy.13 = f32[3072,192]{1,0:T(8,128)} copy(f32[3072,192]{0,1:T(8,128)S(1)} %fusion.13) | data formatting | bytes 4718592
  122.3 0.0 reduce-scatter.4.cloned.1.call-update
  122.3 65.3 %reduce-scatter.4.cloned.1.call-done = f32[192,192]{1,0:T(8,128)} async-done(((f32[3072,192]{1,0:T(8,128)}), f32[192,192]{1,0:T(8,128)}) %reduce-scatter.4.cloned.1.call-update) | async-done | bytes 147472
  187.5 1.7 copy.14
  189.3 3.4 %all-to-all-start.2 = ((f32[192,2,96]{0,2,1:T(8,128)}), f32[192,2,96]{0,2,1:T(8,128)S(1)}, u32[]{:S(2)}, u32[]{:S(2)}) async-start(f32[192,2,96]{0,2,1:T(8,128)} %bitcast.10), calls=%async_computation.2 | async-start | bytes 393216 | tf_op jit(solution)/shard_map/all_to_all | solution.py:73
  192.7 0.1 eq.15
  192.8 4.7 %all-to-all-done.2 = f32[192,2,96]{0,2,1:T(8,128)S(1)} async-done(((f32[192,2,96]{0,2,1:T(8,128)}), f32[192,2,96]{0,2,1:T(8,128)S(1)}, u32[]{:S(2)}, u32[]{:S(2)}) %all-to-all-start.2) | async-done | bytes 147488 | tf_op jit(solution)/shard_map/all_to_all | solution.py:73
  197.5 0.3 fusion.50
  197.8 0.9 fusion.25
  (7 shorter events, 0.0 us)
Async XLA Ops:
  6.5 0.8 copy-start
  6.5 51.0 %all-gather.5.cloned.1.call-start = ((), (), s32[]{:S(2)}) async-start(), calls=%async_computation.5 | async-start | bytes 1671168 | tf_op jit(solution)/shard_map/all_gather | solution.py:43
  17.4 81.0 %all-gather.3.cloned.1.call-start = ((), (), s32[]{:S(2)}) async-start(), calls=%async_computation.4 | async-start | bytes 1671168 | tf_op jit(solution)/shard_map/all_gather | solution.py:44
  27.4 160.2 %reduce-scatter.4.cloned.1.call-start = ((), (), s32[]{:S(2)}) async-start(), calls=%async_computation.6 | async-start | bytes 3342336
  62.3 41.9 %copy-start.2 = (f32[192,1024]{1,0:T(8,128)}, f32[192,1024]{1,0:T(8,128)S(1)}, u32[]{:S(2)}) copy-start(f32[192,1024]{1,0:T(8,128)S(1)} %fusion.2) | copy-start | bytes 2359300
  62.3 41.9 %copy-start.1 = (bf16[192,3072]{0,1:T(8,128)(2,1)S(1)}, bf16[192,3072]{0,1:T(8,128)(2,1)}, u32[]{:S(2)}) copy-start(bf16[192,3072]{0,1:T(8,128)(2,1)} %all-gather.5.cloned.1.call-done) | copy-start | bytes 3538948
  120.0 72.7 %copy-start.3 = (s32[2,96]{1,0:T(2,128)S(1)}, s32[2,96]{1,0:T(2,128)}, u32[]{:S(2)}) copy-start(s32[2,96]{1,0:T(2,128)} %param.13) | copy-start | bytes 2308
  189.3 8.2 %all-to-all-start.2 = ((f32[192,2,96]{0,2,1:T(8,128)}), f32[192,2,96]{0,2,1:T(8,128)S(1)}, u32[]{:S(2)}, u32[]{:S(2)}) async-start(f32[192,2,96]{0,2,1:T(8,128)} %bitcast.10), calls=%async_computation.2 | async-start | bytes 393216 | tf_op jit(solution)/shard_map/all_to_all | solution.py:73
Sparse Core Ops, SparseCore 0:
  17.6 39.9 all-gather.4
  59.8 38.5 all-gather.2
  122.4 65.0 reduce-scatter.3
where the time goes:
time: 206 us; the launch traced here: 205 us
  waiting for transfers between devices  136 us (66%)
  matrix products  27.3 us (13%)
  blocking collectives  15 us (7%)
  between operations  13.2 us (6%)
  local copies, waits for them, and re-layouts  9.05 us (4%)
  starting transfers between devices  3.52 us (2%)
    unnamed x4, waiting for transfers between devices  65.3 us
    all_gather x1, waiting for transfers between devices, body(): part_cot = lax.all_gather(slot_cot, 'hidden', axis=1, tiled=True)  36.2 us
    all_gather x1, waiting for transfers between devices, body(): part_inputs = lax.all_gather(slot_inputs, 'hidden', axis=1, tiled=True)  30.1 us
    dot_general x1, matrix products, body(): lax.dot_general(gate_rows, grad_gate, (((1,), (1,)), ((), ())), preferred...  9.91 us
    all_to_all x1, blocking collectives, body(): lax.all_to_all(chosen, 'expert', split_axis=0, concat_axis=0, tiled=True)  8.33 us
    all_to_all x1, blocking collectives, body(): lax.all_to_all(sent_cot, 'expert', split_axis=0, concat_axis=0, tiled=True)  6.65 us
    dot_general x1, matrix products, body(): lax.dot_general(up_rows, grad_up, (((1,), (1,)), ((), ())), preferred_ele...  5.93 us
    dot_general x1, matrix products, body(): lax.dot_general(part_cot, down_mat, (((1,), (1,)), ((), ())), preferred_e...  5.65 us
  transfers between devices with their start and end apart: 4, of which 4 were waited for; matrix products, arithmetic and copies ran while one was open for 4% of the time, Pallas kernels for 0%

commit v1 on v0

--- a/solution.py
+++ b/solution.py
@@ -40,8 +40,13 @@
     )
     slot_inputs = recv_inputs.reshape(slot_count, -1)
     slot_cot = recv_cot.reshape(slot_count, -1)
-    part_inputs = lax.all_gather(slot_inputs, "hidden", axis=1, tiled=True)
-    part_cot = lax.all_gather(slot_cot, "hidden", axis=1, tiled=True)
+    part_inputs, part_cot = jnp.split(
+        lax.all_gather(
+            jnp.concatenate([slot_inputs, slot_cot], axis=0), "hidden", axis=1, tiled=True
+        ),
+        [slot_inputs.shape[0]],
+        axis=0,
+    )
     gate_rows = gate_mat
     up_rows = up_mat
     gate_pre = jnp.dot(part_inputs, gate_rows, preferred_element_type=jnp.float32)

time: 206 us -> 184 us (0.89)
  waiting for transfers between devices: 136 us -> 119 us
  blocking collectives: 15 us -> 0 us
  starting transfers between devices: 3.52 us -> 11.1 us
    all_gather x2 -> x1, waiting for transfers between devices: 66.3 us -> 43.2 us  [body(): lax.all_gather(jnp.concatenate([slot_inputs, slot_cot], axis=0), 'hidden'...]
    all_to_all x2 -> x0, blocking collectives: 15 us -> none  [the longest x1 8.33 us: body(): lax.all_to_all(chosen, 'expert', split_axis=0, concat_axis=0, tiled=True)]
    all_to_all x0 -> x2, starting transfers between devices: none -> 7.57 us  [the longest x1 4.23 us: body(): lax.all_to_all(sent_cot, 'expert', split_axis=0, concat_axis=0, tiled=True)]
    all_to_all x0 -> x2, waiting for transfers between devices: none -> 6.16 us  [the longest x1 4.13 us: body(): lax.all_to_all(chosen, 'expert', split_axis=0, concat_axis=0, tiled=True)]
    unnamed x10 -> x12, local copies, waits for them, and re-layouts: 4.04 us -> 4.96 us
    unnamed x4 -> x3, waiting for transfers between devices: 65.3 us -> 65.2 us
  transfers between devices with their start and end apart: 4 -> 5, of which waited for: 4 -> 5; matrix products, arithmetic and copies ran while one was open for 4% -> 1% of each run, Pallas kernels for 0% -> 0%
where the time goes in v1:
time: 184 us; the launch traced here: 183 us
  waiting for transfers between devices  119 us (65%)
  matrix products  27.8 us (15%)
  between operations  13.5 us (7%)
  starting transfers between devices  11.1 us (6%)
  local copies, waits for them, and re-layouts  9.32 us (5%)
  other arithmetic  2.2 us (1%)
    unnamed x3, waiting for transfers between devices  65.2 us
    all_gather x1, waiting for transfers between devices, body(): lax.all_gather(jnp.concatenate([slot_inputs, slot_cot], axis=0), 'hidden'...  43.2 us
    dot_general x1, matrix products, body(): lax.dot_general(gate_rows, grad_gate, (((1,), (1,)), ((), ())), preferred...  10.4 us
    dot_general x1, matrix products, body(): lax.dot_general(up_rows, grad_up, (((1,), (1,)), ((), ())), preferred_ele...  5.98 us
    dot_general x1, matrix products, body(): lax.dot_general(part_cot, down_mat, (((1,), (1,)), ((), ())), preferred_e...  5.43 us
    unnamed x12, local copies, waits for them, and re-layouts  4.96 us
    dot_general x1, matrix products, body(): jnp.dot(part_inputs, gate_rows, preferred_element_type=jnp.float32)  4.81 us
    all_to_all x1, waiting for transfers between devices, body(): lax.all_to_all(reduced.reshape(local_width, expert_count, per_source), 'e...  4.72 us
  transfers between devices with their start and end apart: 5, of which 5 were waited for; matrix products, arithmetic and copies ran while one was open for 1% of the time, Pallas kernels for 0%

profile of v1, /device:TPU:0, one launch (start us, length us, event | category | flops | bytes accessed | tf_op | source)
XLA Modules:
  0.0 183.1 jit_solution(10434137969681644414)
XLA Ops:
  6.5 0.8 reshape.59
  7.3 0.0 copy-done
  7.3 1.0 gather_fusion.1
  8.4 1.4 fusion.61
  9.8 4.2 %all-to-all-start.1 = ((bf16[2,96,192]{2,1,0:T(8,128)(2,1)}), bf16[2,96,192]{2,1,0:T(8,128)(2,1)S(1)}, u32[]{:S(2)}, u32[]{:S(2)}) async-start(bf16[2,96,192]{2,1,0:T(8,128)(2,1)} %fusion.61), calls=%async_computation.1 | async-start | bytes 196608 | tf_op jit(solution)/shard_map/all_to_all | solution.py:39
  14.0 2.3 %gather_fusion = bf16[192,192]{1,0:T(8,128)(2,1)} fusion(bf16[96,192]{1,0:T(8,128)(2,1)} %param.8, s32[1024]{0:T(1024)S(1)} %pad_clamp_fusion), kind=kCustom, calls=%fused_computation | custom fusion | bytes 148224 | tf_op jit(solution)/shard_map/gather | solution.py:34
  16.3 2.0 %all-to-all-done.1 = bf16[2,96,192]{2,1,0:T(8,128)(2,1)S(1)} async-done(((bf16[2,96,192]{2,1,0:T(8,128)(2,1)}), bf16[2,96,192]{2,1,0:T(8,128)(2,1)S(1)}, u32[]{:S(2)}, u32[]{:S(2)}) %all-to-all-start.1) | async-done | bytes 73760 | tf_op jit(solution)/shard_map/all_to_all | solution.py:39
  18.3 3.3 %all-to-all-start = ((bf16[2,96,192]{2,1,0:T(8,128)(2,1)}), bf16[2,96,192]{2,1,0:T(8,128)(2,1)S(1)}, u32[]{:S(2)}, u32[]{:S(2)}) async-start(bf16[2,96,192]{2,1,0:T(8,128)(2,1)} %bitcast.1), calls=%async_computation | async-start | bytes 196608 | tf_op jit(solution)/shard_map/all_to_all | solution.py:38
  21.7 0.0 all-gather.2.cloned.1.call-start
  21.7 0.1 copy.12
  21.8 4.1 %all-to-all-done = bf16[2,96,192]{2,1,0:T(8,128)(2,1)S(1)} async-done(((bf16[2,96,192]{2,1,0:T(8,128)(2,1)}), bf16[2,96,192]{2,1,0:T(8,128)(2,1)S(1)}, u32[]{:S(2)}, u32[]{:S(2)}) %all-to-all-start) | async-done | bytes 73760 | tf_op jit(solution)/shard_map/all_to_all | solution.py:38
  26.0 0.1 copy.11
  26.1 0.7 pad_maximum_fusion
  26.8 0.0 all-gather.2.cloned.1.call-update
  26.8 0.0 copy-start.4
  26.9 0.0 reduce-scatter.4.cloned.1.call-start
  26.9 43.2 %all-gather.2.cloned.1.call-done = bf16[384,3072]{0,1:T(8,128)(2,1)} async-done(((bf16[384,192]{0,1:T(8,128)(2,1)}), bf16[384,3072]{0,1:T(8,128)(2,1)}) %all-gather.2.cloned.1.call-update) | async-done | bytes 2359312 | tf_op jit(solution)/shard_map/all_gather | solution.py:44
  70.1 4.8 %fusion.2 = f32[192,1024]{1,0:T(8,128)S(1)} fusion(bf16[1,3072,1024]{2,1,0:T(8,128)(2,1)} %param.10, bf16[384,3072]{0,1:T(8,128)(2,1)} %all-gather.2.cloned.1.call-done), kind=kOutput, calls=%fused_computation.4 | convolution fusion | flops 1207959552 | bytes 8650752 | tf_op jit(solution)/shard_map/dot_general | solution.py:52
  75.0 5.4 %fusion.29 = f32[192,1024]{1,0:T(8,128)S(1)} fusion(bf16[1,1024,3072]{2,1,0:T(8,128)(2,1)} %param.12, bf16[384,3072]{0,1:T(8,128)(2,1)S(1)} %copy-done.3, s32[1,192,1024]{2,1,0:T(8,128)S(1)} %copy-done.4), kind=kOutput, calls=%fused_computation.19 | convolution fusion | flops 1208549376 | bytes 9437184 | tf_op jit(solution)/shard_map/dot_general | solution.py:54
  80.4 0.9 copy-done.1
  81.3 10.4 %fusion = f32[192,3072]{1,0:T(8,128)} fusion(bf16[1,3072,1024]{2,1,0:T(8,128)(2,1)} %param.10, f32[192,1024]{1,0:T(8,128)S(1)} %fusion.2, f32[192,1024]{1,0:T(8,128)S(1)} %fusion.29, bf16[1,3072,1024]{2,1,0:T(8,128)(2,1)} %param.11, bf16[384,3072]{0,1:T(8,128)(2,1)} %all-gather.2.cloned.1.call-done), kind=kOutput, calls=%fused_computation.2 | convolution fusion | flops 2420047872 | bytes 18087936 | tf_op jit(solution)/shard_map/dot_general | solution.py:68
  91.7 6.0 %fusion.13 = f32[3072,192]{0,1:T(8,128)S(1)} fusion(f32[192,3072]{1,0:T(8,128)} %fusion, bf16[1,3072,1024]{2,1,0:T(8,128)(2,1)} %param.11, f32[192,1024]{1,0:T(8,128)} %copy-done.1, f32[192,1024]{1,0:T(8,128)S(1)} %fusion.2), kind=kOutput, calls=%fused_computation.13 | convolution fusion | flops 1210515456 | bytes 12582912 | tf_op jit(solution)/shard_map/dot_general | solution.py:71
  97.6 2.3 %copy.13 = f32[3072,192]{1,0:T(8,128)} copy(f32[3072,192]{0,1:T(8,128)S(1)} %fusion.13) | data formatting | bytes 4718592
  99.9 0.0 reduce-scatter.4.cloned.1.call-update
  100.0 65.1 %reduce-scatter.4.cloned.1.call-done = f32[192,192]{1,0:T(8,128)} async-done(((f32[3072,192]{1,0:T(8,128)}), f32[192,192]{1,0:T(8,128)}) %reduce-scatter.4.cloned.1.call-update) | async-done | bytes 147472
  165.1 1.7 copy.14
  166.8 3.4 %all-to-all-start.2 = ((f32[192,2,96]{0,2,1:T(8,128)}), f32[192,2,96]{0,2,1:T(8,128)S(1)}, u32[]{:S(2)}, u32[]{:S(2)}) async-start(f32[192,2,96]{0,2,1:T(8,128)} %bitcast.10), calls=%async_computation.2 | async-start | bytes 393216 | tf_op jit(solution)/shard_map/all_to_all | solution.py:78
  170.3 0.0 copy-done.2
  170.3 0.1 eq.15
  170.4 4.7 %all-to-all-done.2 = f32[192,2,96]{0,2,1:T(8,128)S(1)} async-done(((f32[192,2,96]{0,2,1:T(8,128)}), f32[192,2,96]{0,2,1:T(8,128)S(1)}, u32[]{:S(2)}, u32[]{:S(2)}) %all-to-all-start.2) | async-done | bytes 147488 | tf_op jit(solution)/shard_map/all_to_all | solution.py:78
  175.1 0.3 fusion.63
  175.4 0.9 fusion.34
  (9 shorter events, 0.0 us)
Async XLA Ops:
  6.5 0.8 copy-start
  9.8 8.6 %all-to-all-start.1 = ((bf16[2,96,192]{2,1,0:T(8,128)(2,1)}), bf16[2,96,192]{2,1,0:T(8,128)(2,1)S(1)}, u32[]{:S(2)}, u32[]{:S(2)}) async-start(bf16[2,96,192]{2,1,0:T(8,128)(2,1)} %fusion.61), calls=%async_computation.1 | async-start | bytes 196608 | tf_op jit(solution)/shard_map/all_to_all | solution.py:39
  18.3 7.6 %all-to-all-start = ((bf16[2,96,192]{2,1,0:T(8,128)(2,1)}), bf16[2,96,192]{2,1,0:T(8,128)(2,1)S(1)}, u32[]{:S(2)}, u32[]{:S(2)}) async-start(bf16[2,96,192]{2,1,0:T(8,128)(2,1)} %bitcast.1), calls=%async_computation | async-start | bytes 196608 | tf_op jit(solution)/shard_map/all_to_all | solution.py:38
  21.7 48.4 %all-gather.2.cloned.1.call-start = ((), (), s32[]{:S(2)}) async-start(), calls=%async_computation.4 | async-start | bytes 2506752 | tf_op jit(solution)/shard_map/all_gather | solution.py:44
  26.8 48.1 %copy-start.4 = (s32[1,192,1024]{2,1,0:T(8,128)S(1)}, s32[1,192,1024]{2,1,0:T(8,128)}, u32[]{:S(2)}) copy-start(s32[1,192,1024]{2,1,0:T(8,128)} %param.15) | copy-start | bytes 2359300
  26.9 138.3 %reduce-scatter.4.cloned.1.call-start = ((), (), s32[]{:S(2)}) async-start(), calls=%async_computation.5 | async-start | bytes 3342336
  70.1 4.8 %copy-start.3 = (bf16[384,3072]{0,1:T(8,128)(2,1)S(1)}, bf16[384,3072]{0,1:T(8,128)(2,1)}, u32[]{:S(2)}) copy-start(bf16[384,3072]{0,1:T(8,128)(2,1)} %all-gather.2.cloned.1.call-done) | copy-start | bytes 7077892
  80.4 0.9 copy-start.1
  99.9 70.3 %copy-start.2 = (s32[2,96]{1,0:T(2,128)S(1)}, s32[2,96]{1,0:T(2,128)}, u32[]{:S(2)}) copy-start(s32[2,96]{1,0:T(2,128)} %param.13) | copy-start | bytes 2308
  166.8 8.2 %all-to-all-start.2 = ((f32[192,2,96]{0,2,1:T(8,128)}), f32[192,2,96]{0,2,1:T(8,128)S(1)}, u32[]{:S(2)}, u32[]{:S(2)}) async-start(f32[192,2,96]{0,2,1:T(8,128)} %bitcast.10), calls=%async_computation.2 | async-start | bytes 393216 | tf_op jit(solution)/shard_map/all_to_all | solution.py:78
Sparse Core Ops, SparseCore 0:
  27.0 43.1 all-gather.1
  100.1 64.9 reduce-scatter.3
